TPU v7x, 512 devices: a whole 4x4x16 slice. The times are simulated.
512 devices in a mesh: dp: 4 (over x), ctx: 16 (over z), mp: 8 (over y, core).
Axes of the slice: x: 4, y: 4, z: 16, core: 2. Of those that a mesh axis runs over, the one named last changes fastest.
Arguments:
- tokens: bfloat16 [4, 2048, 4096], P('dp', 'ctx'), may hold values from -52 to 52
- x_weight: bfloat16 [4096, 8192], P(('dp', 'ctx'), 'mp'), may hold values from -0.09375 to 0.09375
- bc_weight: bfloat16 [4096, 1024], P(('dp', 'ctx'), 'mp'), may hold values from -0.09375 to 0.09375
- dt_weight: bfloat16 [4096, 128], P(('dp', 'ctx'), 'mp'), may hold values from -0.0234375 to 0.0234375
- conv_x: float32 [5, 8192], P(None, 'mp'), may hold values from -0.5 to 0.5
- conv_bc: float32 [5, 1024], P(None, 'mp'), may hold values from -0.5 to 0.5
- dt_bias: float32 [128], P('mp'), may hold values from -4.5 to -2.5
- a_log: float32 [128], P('mp')
- d_skip: float32 [128], P('mp'), may hold values from 0.5 to 1.5
- norm_gain: float32 [8192], P('mp'), may hold values from 0.5 to 1.5
Outputs:
- mixer_out: bfloat16 [4, 2048, 8192], P('dp', 'ctx', 'mp')
- kurtosis: float32 [4096], P('mp')
All inputs are finite; a program needn't handle non-finite values.
Results may differ from a plain program's by a relative error of at most 0.015.
Values may be sent and summed in bfloat16 or wider, within the bound.
No kernel may reach another device: no remote copies, remote signals or barrier semaphores. Data moves between devices by JAX's collectives and lax.ppermute only.
A program may use at most 64 MiB of HBM per device.

v0:
```python
import jax
import jax.numpy as jnp
from jax import lax
from jax.sharding import PartitionSpec as P

ROOT = 64
HEADS = 128
G = 4
NS = 128
HIGH = lax.Precision.HIGHEST


def passed_along(value, axis, steps):
    count = lax.axis_size(axis)
    first, last = (max(0, -steps), min(count, count - steps))
    return lax.ppermute(value, axis, [(source, source + steps) for source in range(first, last)])


def entering(decay, contrib, axis):
    length, place = (lax.axis_size(axis), lax.axis_index(axis))
    lanes = contrib.shape[-1]
    rows = contrib.size // lanes
    tail = jnp.zeros((8, lanes), jnp.float32).at[0, : decay.size].set(decay.reshape(-1))
    flat = jnp.concatenate([contrib.reshape(rows, lanes), tail]).astype(jnp.bfloat16)
    everything = lax.all_gather(flat, axis).astype(jnp.float32)
    states = everything[:, :rows].reshape((length,) + contrib.shape)
    decays = everything[:, rows, : decay.size].reshape((length,) + decay.shape)
    source = lax.broadcasted_iota(jnp.int32, (length, length), 0)
    between = lax.broadcasted_iota(jnp.int32, (length, length), 1)
    inside = jnp.logical_and(between > source, between < place)
    factors = jnp.where(inside[:, :, None, None], decays[None], 1.0)
    weights = jnp.prod(factors, 1)
    weights = jnp.where((source[:, 0] < place)[:, None, None], weights, 0.0)
    return jnp.einsum("jgh,jghpn->ghpn", weights, states, precision=HIGH)


def hadamard_signs(sign_order):
    row_index = lax.broadcasted_iota(jnp.int32, (sign_order, sign_order), 0)
    col_index = lax.broadcasted_iota(jnp.int32, (sign_order, sign_order), 1)
    common = jnp.bitwise_and(row_index, col_index)
    parity = jnp.zeros((sign_order, sign_order), jnp.int32)
    for bit_index in range(sign_order.bit_length() - 1):
        parity = parity + jnp.bitwise_and(jnp.right_shift(common, bit_index), 1)
    return 1.0 - 2.0 * jnp.bitwise_and(parity, 1).astype(jnp.float32)


def kurtosis_from(powers, row_count):
    average = powers[0] / row_count
    second = powers[1] / row_count - average * average
    fourth = (
        powers[3] / row_count
        - 4.0 * average * powers[2] / row_count
        + 6.0 * average * average * powers[1] / row_count
        - 3.0 * average * average * average * average
    )
    return fourth / (second * second + 1e-06)


def shards(
    tokens, x_weight, bc_weight, dt_weight, conv_x, conv_bc, dt_bias, a_log, d_skip, norm_gain
):
    tok_rows = tokens.shape[1]
    model_width = tokens.shape[2]
    signs = hadamard_signs(ROOT)
    blocks = tokens.reshape(tok_rows, ROOT, ROOT)
    first_pass = jnp.einsum(
        "tab,ac->tcb", blocks, signs.astype(jnp.bfloat16), preferred_element_type=jnp.float32
    )
    second = jnp.einsum("tcb,bd->tcd", first_pass, signs, precision=HIGH)
    rotated = (second.reshape(tok_rows, model_width) / ROOT).astype(jnp.bfloat16)
    channel_share = model_width // lax.axis_size("mp")
    own_cols = lax.dynamic_slice_in_dim(
        rotated, lax.axis_index("mp") * channel_share, channel_share, 1
    ).astype(jnp.float32)
    square = own_cols * own_cols
    powers = jnp.stack(
        [
            jnp.sum(own_cols, 0),
            jnp.sum(square, 0),
            jnp.sum(square * own_cols, 0),
            jnp.sum(square * square, 0),
        ]
    )
    row_count = float(tok_rows * lax.axis_size("dp") * lax.axis_size("ctx"))
    totals = lax.psum(lax.psum(powers, "ctx"), "dp")
    totals, rotated = lax.optimization_barrier((totals, rotated))
    kurtosis = kurtosis_from(totals, row_count)
    local_panel = jnp.concatenate([x_weight, bc_weight, dt_weight], 1)
    panel = lax.all_gather(local_panel, ("dp", "ctx"), axis=0, tiled=True)
    both = jnp.dot(rotated, panel, preferred_element_type=jnp.float32)
    x_end = x_weight.shape[1]
    bc_end = x_end + bc_weight.shape[1]
    projected = (both[:, :x_end], both[:, x_end:bc_end], both[:, bc_end:])
    x_cols = x_weight.shape[1]
    joined = jnp.concatenate(
        [projected[0].astype(jnp.bfloat16), projected[1].astype(jnp.bfloat16)], 1
    )
    dt_proj = lax.optimization_barrier(projected[2].astype(jnp.bfloat16))
    conv_taps = jnp.concatenate([conv_x, conv_bc], 1)
    kernel = conv_taps.shape[0] - 1
    rim_rows = passed_along(joined[tok_rows - (kernel - 1) :], "ctx", 1)
    padded = jnp.concatenate([rim_rows, joined], 0)
    conv_sum = conv_taps[kernel]
    for tap_index in range(kernel):
        conv_sum = conv_sum + conv_taps[tap_index] * padded[tap_index : tap_index + tok_rows]
    convolved = jax.nn.silu(conv_sum).astype(jnp.bfloat16)
    x_conv = convolved[:, :x_cols]
    group_all = lax.all_gather(convolved[:, x_cols:], "mp", axis=1, tiled=True)
    heads_dev = dt_weight.shape[1]
    head_size = x_cols // heads_dev
    per_group = HEADS // G
    groups_here = max(1, heads_dev // per_group)
    heads_local = heads_dev // groups_here
    first_group = lax.axis_index("mp") * heads_dev // per_group
    write_all = group_all[:, : G * NS].reshape(tok_rows, G, NS)
    read_all = group_all[:, G * NS :].reshape(tok_rows, G, NS)
    write_here = lax.dynamic_slice_in_dim(write_all, first_group, groups_here, 1)
    read_here = lax.dynamic_slice_in_dim(read_all, first_group, groups_here, 1)
    step_size = jax.nn.softplus(dt_proj.astype(jnp.float32) + dt_bias)
    decay_rate = step_size * jnp.exp(a_log)
    cumulative = jnp.cumsum(decay_rate, 0)
    block_end = cumulative[-1]
    causal = lax.broadcasted_iota(jnp.int32, (tok_rows, tok_rows), 0) >= lax.broadcasted_iota(
        jnp.int32, (tok_rows, tok_rows), 1
    )
    spread = cumulative.T[:, :, None] - cumulative.T[:, None, :]
    decay_mask = jnp.where(causal, jnp.exp(-jnp.where(causal, spread, 0.0)), 0.0)
    scores = jnp.einsum("tgn,sgn->gts", read_here, write_here, preferred_element_type=jnp.float32)
    weights = (
        scores[:, None]
        * decay_mask.reshape(groups_here, heads_local, tok_rows, tok_rows)
        * step_size.T.reshape(groups_here, heads_local, 1, tok_rows)
    ).astype(jnp.bfloat16)
    x_heads = x_conv.reshape(tok_rows, groups_here, heads_local, head_size)
    within_block = jnp.einsum(
        "ghts,sghp->tghp", weights, x_heads, preferred_element_type=jnp.float32
    )
    update = (
        (jnp.exp(-(block_end - cumulative)) * step_size).reshape(
            tok_rows, groups_here, heads_local
        )[..., None]
        * x_heads
    ).astype(jnp.bfloat16)
    contrib = jnp.einsum("sghp,sgn->ghpn", update, write_here, preferred_element_type=jnp.float32)
    carried = entering(jnp.exp(-block_end).reshape(groups_here, heads_local), contrib, "ctx")
    from_before = jnp.exp(-cumulative).reshape(tok_rows, groups_here, heads_local)[
        ..., None
    ] * jnp.einsum("tgn,ghpn->tghp", read_here.astype(jnp.float32), carried, precision=HIGH)
    output_raw = (
        within_block
        + from_before
        + d_skip.reshape(groups_here, heads_local)[None, :, :, None] * x_heads.astype(jnp.float32)
    )
    mean_square = jnp.mean(output_raw * output_raw, -1, keepdims=True)
    normed = (
        output_raw
        * lax.rsqrt(mean_square + 1e-05)
        * norm_gain.reshape(groups_here, heads_local, head_size)
    )
    return (normed.reshape(1, tok_rows, x_cols).astype(jnp.bfloat16), kurtosis)


def solution(mesh):
    return jax.shard_map(
        shards,
        mesh=mesh,
        in_specs=(
            P("dp", "ctx", None),
            P(("dp", "ctx"), "mp"),
            P(("dp", "ctx"), "mp"),
            P(("dp", "ctx"), "mp"),
            P(None, "mp"),
            P(None, "mp"),
            P("mp"),
            P("mp"),
            P("mp"),
            P("mp"),
        ),
        out_specs=(P("dp", "ctx", "mp"), P("mp")),
        check_vma=False,
    )
```

profile of v0, /device:TPU:4, one launch (start us, length us, event | category | flops | bytes accessed | tf_op | source)
XLA Modules:
  0.0 302.1 jit_solution(1857820000837005802)
XLA Ops:
  7.2 0.0 all-gather.3.cloned.1.call-start
  7.2 0.8 copy.43
  8.0 1.6 pad_maximum_fusion.1
  9.6 0.0 all-gather.3.cloned.1.call-update
  9.6 0.0 all-gather.5.cloned.1.call-start
  9.7 0.0 copy-start.5
  9.7 0.0 copy-start.1
  9.7 0.0 copy-start.3
  9.7 1.6 copy.40
  11.3 0.9 convolution_bitcast_fusion
  12.2 3.3 %multiply_convert_fusion = bf16[128,64,64]{0,2,1:T(8,128)(2,1)S(1)} fusion(f32[128,64,64]{0,1,2:T(8,128)S(1)} %convolution_bitcast_fusion), kind=kOutput, calls=%fused_computation.5 | convolution fusion | flops 403791872 | bytes 3145728 | tf_op jit(solution)/shard_map/tcb,bd->tcd/dot_general | solution.py:69
  15.6 0.3 convert_reduce_fusion
  15.9 37.2 %psum.14 = f32[4,512]{1,0:T(4,128)S(1)} all-reduce(f32[4,512]{1,0:T(4,128)S(1)} %pad_maximum_fusion.2), channel_id=1, replica_groups=mesh['dp'=4,'ctx'=16,'mp'=8] {'ctx'}, use_global_device_ids=true, to_apply=%region_4.0 | all-reduce | flops 2048 | bytes 16384 | tf_op jit(solution)/shard_map/psum | solution.py:85
  53.1 8.4 %psum.15 = f32[4,512]{1,0:T(4,128)S(1)} all-reduce(f32[4,512]{1,0:T(4,128)S(1)} %psum.14), channel_id=1, replica_groups=mesh['dp'=4,'ctx'=16,'mp'=8] {'dp'}, use_global_device_ids=true, to_apply=%region_5.0 | all-reduce | flops 2048 | bytes 16384 | tf_op jit(solution)/shard_map/psum | solution.py:85
  61.6 0.1 slice_reduce_fusion.4
  61.7 0.0 copy-start.4
  61.7 116.0 %all-gather.3.cloned.1.call-done = bf16[4096,1168]{1,0:T(8,128)(2,1)} async-done(((bf16[64,1168]{1,0:T(8,128)(2,1)}), bf16[4096,1168]{1,0:T(8,128)(2,1)}) %all-gather.3.cloned.1.call-update) | async-done | bytes 9568272 | tf_op jit(solution)/shard_map/all_gather | solution.py:89
  177.7 8.0 %convolution_convert_fusion = bf16[128,1168]{0,1:T(8,128)(2,1)S(1)} fusion(bf16[128,4096]{0,1:T(8,128)(2,1)S(1)} %bitcast.81, bf16[4096,1168]{1,0:T(8,128)(2,1)} %all-gather.3.cloned.1.call-done), kind=kOutput, calls=%fused_computation.2 | convolution fusion | flops 1224886272 | bytes 10915840 | tf_op jit(solution)/shard_map/dot_general | solution.py:90
  185.7 0.1 slice.121
  185.9 0.1 broadcast_multiply_fusion
  186.0 0.1 copy.45
  186.1 0.2 reduce_window_sum.11
  186.2 0.1 copy.49
  186.3 3.3 %collective-permute-start = (bf16[3,1152]{0,1:T(8,128)(2,1)S(1)}, bf16[3,1152]{0,1:T(8,128)(2,1)S(1)}, u32[]{:S(2)}, u32[]{:S(2)}) collective-permute-start(bf16[3,1152]{0,1:T(8,128)(2,1)S(1)} %slice.121), channel_id=1, source_target_pairs={{0,8},{8,16},{16,24},{24,32},{32,40},{40,48},{48,56},{56,64},{64,7... | collective-permute-start | bytes 20744 | tf_op jit(solution)/shard_map/ppermute | solution.py:16
  189.6 0.1 fusion.60
  189.7 4.1 %collective-permute-done = bf16[3,1152]{0,1:T(8,128)(2,1)S(1)} collective-permute-done((bf16[3,1152]{0,1:T(8,128)(2,1)S(1)}, bf16[3,1152]{0,1:T(8,128)(2,1)S(1)}, u32[]{:S(2)}, u32[]{:S(2)}) %collective-permute-start) | collective-permute-done | bytes 6944 | tf_op jit(solution)/shard_map/ppermute | solution.py:16
  193.8 1.4 multiply_convert_fusion.2
  195.2 13.4 %all_gather.11 = bf16[128,1024]{0,1:T(8,128)(2,1)S(1)} all-gather(bf16[128,128]{0,1:T(8,128)(2,1)S(1)} %slice.131), channel_id=1, replica_groups=mesh['dp'=4,'ctx'=16,'mp'=8] {'mp'}, dimensions={1}, use_global_device_ids=true | all-gather | bytes 294912 | tf_op jit(solution)/shard_map/all_gather | solution.py:108
  208.6 0.1 multiply_convert_fusion.5
  208.7 0.2 fusion.9
  208.9 0.7 fusion.22
  209.7 0.0 all-gather.5.cloned.1.call-update
  209.7 0.1 mul.242
  209.8 0.6 fusion.39
  210.5 0.1 copy.48
  210.5 0.1 copy.46
  210.6 0.2 fusion.26
  210.8 75.6 %all-gather.5.cloned.1.call-done = bf16[16,1032,128]{2,1,0:T(8,128)(2,1)} async-done(((bf16[1,1032,128]{2,1,0:T(8,128)(2,1)}), bf16[16,1032,128]{2,1,0:T(8,128)(2,1)}) %all-gather.5.cloned.1.call-update) | async-done | bytes 4227088 | tf_op jit(solution)/shard_map/all_gather | solution.py:25
  286.3 0.8 slice_convert_fusion
  287.1 0.1 select_reduce_fusion
  287.2 0.1 select_bitcast_fusion
  287.3 0.1 copy.51
  287.4 2.2 slice-done
  289.6 3.6 %fusion = f32[16,1,64,128]{3,1,2,0:T(1,128)S(1)} fusion(f32[16,16,1,1]{0,2,3,1:T(1,128)S(1)} %copy.51, bf16[16,16,64,128]{3,2,1,0:T(8,128)(2,1)S(1)} %bitcast.79), kind=kOutput, calls=%fused_computation | convolution fusion | flops 25165824 | bytes 4719616 | tf_op jit(solution)/shard_map/jgh,jghpn->ghpn/dot_general | solution.py:34
  293.1 0.4 fusion.8
  293.5 0.6 multiply_reduce_fusion
  294.2 0.2 multiply_convert_fusion.4
  294.4 0.9 copy.50
  (29 shorter events, 0.2 us)
Async XLA Ops:
  7.2 170.5 %all-gather.3.cloned.1.call-start = ((), (), s32[]{:S(2)}) async-start(), calls=%async_computation | async-start | bytes 10649600 | tf_op jit(solution)/shard_map/all_gather | solution.py:89
  9.6 276.7 %all-gather.5.cloned.1.call-start = ((), (), s32[]{:S(2)}) async-start(), calls=%async_computation.1 | async-start | bytes 4491264 | tf_op jit(solution)/shard_map/all_gather | solution.py:25
  9.7 51.8 %copy-start.5 = (f32[16]{0:T(128)S(1)}, f32[16]{0:T(128)}, u32[]{:S(2)}) copy-start(f32[16]{0:T(128)} %param.19) | copy-start | bytes 196
  9.7 51.9 %copy-start.1 = (f32[5,1024]{1,0:T(8,128)S(1)}, f32[5,1024]{1,0:T(8,128)}, u32[]{:S(2)}) copy-start(f32[5,1024]{1,0:T(8,128)} %param.16) | copy-start | bytes 61444
  9.7 51.9 %copy-start.3 = (f32[5,128]{1,0:T(8,128)S(1)}, f32[5,128]{1,0:T(8,128)}, u32[]{:S(2)}) copy-start(f32[5,128]{1,0:T(8,128)} %param.17) | copy-start | bytes 7684
  61.7 124.2 %copy-start.4 = (f32[16]{0:T(128)S(1)}, f32[16]{0:T(128)}, u32[]{:S(2)}) copy-start(f32[16]{0:T(128)} %param.18) | copy-start | bytes 196
  185.7 24.0 %copy-start.2 = (f32[1024]{0:T(1024)S(1)}, f32[1024]{0:T(1024)}, u32[]{:S(2)}) copy-start(f32[1024]{0:T(1024)} %param.21) | copy-start | bytes 12292
  186.3 7.5 %collective-permute-start = (bf16[3,1152]{0,1:T(8,128)(2,1)S(1)}, bf16[3,1152]{0,1:T(8,128)(2,1)S(1)}, u32[]{:S(2)}, u32[]{:S(2)}) collective-permute-start(bf16[3,1152]{0,1:T(8,128)(2,1)S(1)} %slice.121), channel_id=1, source_target_pairs={{0,8},{8,16},{16,24},{24,32},{32,40},{40,48},{48,56},{56,64},{64,7... | collective-permute-start | bytes 20744 | tf_op jit(solution)/shard_map/ppermute | solution.py:16
  195.2 92.2 %copy-start = (bf16[128,1152]{0,1:T(8,128)(2,1)}, bf16[128,1152]{0,1:T(8,128)(2,1)S(1)}, u32[]{:S(2)}) copy-start(bf16[128,1152]{0,1:T(8,128)(2,1)S(1)} %multiply_convert_fusion.2) | copy-start | bytes 884740
  287.4 2.2 slice-start
  287.4 6.1 %copy-start.6 = (f32[16]{0:T(128)S(1)}, f32[16]{0:T(128)}, u32[]{:S(2)}) copy-start(f32[16]{0:T(128)} %param.20) | copy-start | bytes 196
  289.6 4.0 %slice-start.1 = ((bf16[128,1152]{0,1:T(8,128)(2,1)}), bf16[128,1024]{0,1:T(8,128)(2,1)S(1)}, s32[]{:S(2)}) async-start(bf16[128,1152]{0,1:T(8,128)(2,1)} %copy-done), calls=%async_computation.3 | async-start | bytes 524288 | tf_op jit(solution)/shard_map/slice | solution.py:107
Sparse Core Ops, SparseCore 0:
  11.5 166.0 all-gather.2
  209.8 76.4 all-gather.4
where the time goes:
time: 302 us
  waiting for transfers between devices  196 us (65%)
  blocking collectives  58.9 us (20%)
  matrix products  17.2 us (6%)
  between operations  14.4 us (5%)
  other arithmetic  6.37 us (2%)
  local copies, waits for them, and re-layouts  6.17 us (2%)
  starting transfers between devices  3.33 us (1%)
    all_gather x1, waiting for transfers between devices, shards(): panel = lax.all_gather(local_panel, ('dp', 'ctx'), axis=0, tiled=True)  116 us
    all_gather x1, waiting for transfers between devices, entering(): everything = lax.all_gather(flat, axis).astype(jnp.float32)  75.6 us
    psum x2, blocking collectives, shards(): totals = lax.psum(lax.psum(powers, 'ctx'), 'dp')  45.6 us
    all_gather x1, blocking collectives, shards(): group_all = lax.all_gather(convolved[:, x_cols:], 'mp', axis=1, tiled=True)  13.4 us
    dot_general x1, matrix products, shards(): both = jnp.dot(rotated, panel, preferred_element_type=jnp.float32)  8.01 us
  transfers between devices with their start and end apart: 3, of which 3 were waited for; matrix products, arithmetic and copies ran while one was open for 2% of the time, Pallas kernels for 0%

commit v1 on v0

--- a/solution.py
+++ b/solution.py
@@ -8,6 +8,28 @@
 G = 4
 NS = 128
 HIGH = lax.Precision.HIGHEST
+
+
+def laid_out(tiles, dim):
+    dims = list(tiles.shape[1:])
+    dims[dim] *= tiles.shape[0]
+    return jnp.moveaxis(tiles, 0, dim).reshape(dims)
+
+
+def gather_around(array, axis, dim):
+    size = lax.axis_size(axis)
+    pairs = [(i, (i + 1) % size) for i in range(size)]
+    back = [(b, a) for a, b in pairs]
+    lower, upper = ([], [])
+    for step in range(size - 1):
+        if step % 2 == 0:
+            lower.append(lax.ppermute(lower[-1] if lower else array, axis, pairs))
+        else:
+            upper.append(lax.ppermute(upper[-1] if upper else array, axis, back))
+    blocks = jnp.stack([*lower[::-1], array, *upper])
+    shift = lax.axis_index(axis) - len(lower)
+    blocks = blocks[(jnp.arange(size) - shift) % size]
+    return laid_out(blocks, dim)
 
 
 def passed_along(value, axis, steps):
@@ -105,7 +127,7 @@
         conv_sum = conv_sum + conv_taps[tap_index] * padded[tap_index : tap_index + tok_rows]
     convolved = jax.nn.silu(conv_sum).astype(jnp.bfloat16)
     x_conv = convolved[:, :x_cols]
-    group_all = lax.all_gather(convolved[:, x_cols:], "mp", axis=1, tiled=True)
+    group_all = gather_around(convolved[:, x_cols:], "mp", 1)
     heads_dev = dt_weight.shape[1]
     head_size = x_cols // heads_dev
     per_group = HEADS // G

time: 302 us -> 308 us (1.020)
  blocking collectives: 58.9 us -> 45.6 us
  starting transfers between devices: 3.33 us -> 12.4 us
  waiting for transfers between devices: 196 us -> 205 us
    all_gather x1 -> x0, blocking collectives: 13.4 us -> none  [shards(): group_all = lax.all_gather(convolved[:, x_cols:], 'mp', axis=1, tiled=True)]
    ppermute x0 -> x7, starting transfers between devices: none -> 8.92 us  [the longest x3 8.89 us: gather_around(): upper.append(lax.ppermute(upper[-1] if upper else array, axis, back))]
    ppermute x0 -> x7, waiting for transfers between devices: none -> 8.71 us  [the longest x4 8.63 us: gather_around(): lower.append(lax.ppermute(lower[-1] if lower else array, axis, pairs))]
  transfers between devices with their start and end apart: 3 -> 10, of which waited for: 3 -> 7; matrix products, arithmetic and copies ran while one was open for 2% -> 3% of each run, Pallas kernels for 0% -> 0%
where the time goes in v1:
time: 308 us
  waiting for transfers between devices  205 us (67%)
  blocking collectives  45.6 us (15%)
  matrix products  17.2 us (6%)
  between operations  14.5 us (5%)
  starting transfers between devices  12.4 us (4%)
  local copies, waits for them, and re-layouts  6.83 us (2%)
  other arithmetic  6.39 us (2%)
    all_gather x1, waiting for transfers between devices, shards(): panel = lax.all_gather(local_panel, ('dp', 'ctx'), axis=0, tiled=True)  116 us
    all_gather x1, waiting for transfers between devices, entering(): everything = lax.all_gather(flat, axis).astype(jnp.float32)  76.1 us
    psum x2, blocking collectives, shards(): totals = lax.psum(lax.psum(powers, 'ctx'), 'dp')  45.6 us
    ppermute x3, starting transfers between devices, gather_around(): upper.append(lax.ppermute(upper[-1] if upper else array, axis, back))  8.89 us
    ppermute x4, waiting for transfers between devices, gather_around(): lower.append(lax.ppermute(lower[-1] if lower else array, axis, pairs))  8.63 us
    dot_general x1, matrix products, shards(): both = jnp.dot(rotated, panel, preferred_element_type=jnp.float32)  8.01 us
  transfers between devices with their start and end apart: 10, of which 7 were waited for; matrix products, arithmetic and copies ran while one was open for 3% of the time, Pallas kernels for 0%

profile of v1, /device:TPU:4, one launch (start us, length us, event | category | flops | bytes accessed | tf_op | source)
XLA Modules:
  0.0 307.7 jit_solution(195308883103428076)
XLA Ops:
  7.2 0.8 copy.43
  8.0 1.6 pad_maximum_fusion.1
  9.7 1.6 copy.40
  11.3 0.9 convolution_bitcast_fusion
  12.2 3.3 %multiply_convert_fusion = bf16[128,64,64]{0,2,1:T(8,128)(2,1)S(1)} fusion(f32[128,64,64]{0,1,2:T(8,128)S(1)} %convolution_bitcast_fusion), kind=kOutput, calls=%fused_computation.6 | convolution fusion | flops 403791872 | bytes 3145728 | tf_op jit(solution)/shard_map/tcb,bd->tcd/dot_general | solution.py:91
  15.5 0.3 convert_reduce_fusion
  15.9 37.2 %psum.14 = f32[4,512]{1,0:T(4,128)S(1)} all-reduce(f32[4,512]{1,0:T(4,128)S(1)} %pad_maximum_fusion.2), channel_id=1, replica_groups=mesh['dp'=4,'ctx'=16,'mp'=8] {'ctx'}, use_global_device_ids=true, to_apply=%region_4.0 | all-reduce | flops 2048 | bytes 16384 | tf_op jit(solution)/shard_map/psum | solution.py:107
  53.1 8.4 %psum.15 = f32[4,512]{1,0:T(4,128)S(1)} all-reduce(f32[4,512]{1,0:T(4,128)S(1)} %psum.14), channel_id=1, replica_groups=mesh['dp'=4,'ctx'=16,'mp'=8] {'dp'}, use_global_device_ids=true, to_apply=%region_5.0 | all-reduce | flops 2048 | bytes 16384 | tf_op jit(solution)/shard_map/psum | solution.py:107
  61.5 0.1 slice_reduce_fusion.4
  61.6 116.0 %all-gather.3.cloned.1.call-done = bf16[4096,1168]{1,0:T(8,128)(2,1)} async-done(((bf16[64,1168]{1,0:T(8,128)(2,1)}), bf16[4096,1168]{1,0:T(8,128)(2,1)}) %all-gather.3.cloned.1.call-update) | async-done | bytes 9568272 | tf_op jit(solution)/shard_map/all_gather | solution.py:111
  177.7 8.0 %convolution_convert_fusion = bf16[128,1168]{0,1:T(8,128)(2,1)S(1)} fusion(bf16[128,4096]{0,1:T(8,128)(2,1)S(1)} %bitcast.102, bf16[4096,1168]{1,0:T(8,128)(2,1)} %all-gather.3.cloned.1.call-done), kind=kOutput, calls=%fused_computation.3 | convolution fusion | flops 1224886272 | bytes 10915840 | tf_op jit(solution)/shard_map/dot_general | solution.py:112
  185.7 0.1 slice.123
  185.8 3.4 %collective-permute-start = (bf16[3,1152]{0,1:T(8,128)(2,1)S(1)}, bf16[3,1152]{0,1:T(8,128)(2,1)S(1)}, u32[]{:S(2)}, u32[]{:S(2)}) collective-permute-start(bf16[3,1152]{0,1:T(8,128)(2,1)S(1)} %slice.123), channel_id=1, source_target_pairs={{0,8},{8,16},{16,24},{24,32},{32,40},{40,48},{48,56},{56,64},{64,7... | collective-permute-start | bytes 20744 | tf_op jit(solution)/shard_map/ppermute | solution.py:38
  189.4 3.9 %collective-permute-done = bf16[3,1152]{0,1:T(8,128)(2,1)S(1)} collective-permute-done((bf16[3,1152]{0,1:T(8,128)(2,1)S(1)}, bf16[3,1152]{0,1:T(8,128)(2,1)S(1)}, u32[]{:S(2)}, u32[]{:S(2)}) %collective-permute-start) | collective-permute-done | bytes 6944 | tf_op jit(solution)/shard_map/ppermute | solution.py:38
  193.3 1.4 multiply_convert_fusion.2
  194.8 0.1 broadcast_multiply_fusion
  194.9 0.1 copy.45
  195.0 0.2 reduce_window_sum.11
  195.2 4.2 %collective-permute-done.1 = bf16[128,128]{0,1:T(8,128)(2,1)S(1)} collective-permute-done((bf16[128,128]{0,1:T(8,128)(2,1)S(1)}, bf16[128,128]{0,1:T(8,128)(2,1)S(1)}, u32[]{:S(2)}, u32[]{:S(2)}) %collective-permute-start.1) | collective-permute-done | bytes 32800 | tf_op jit(solution)/shard_map/ppermute | solution.py:26
  199.3 0.1 copy.49
  199.4 3.0 collective-permute-start.5
  202.4 1.5 collective-permute-done.2
  203.9 0.1 fusion.62
  204.0 3.0 collective-permute-start.6
  207.0 1.5 collective-permute-done.3
  208.4 0.1 multiply_convert_fusion.5
  208.5 0.0 collective-permute-done.6
  208.6 3.0 collective-permute-start.7
  211.5 1.5 collective-permute-done.4
  213.1 0.6 gather_fusion
  213.7 0.2 fusion.9
  214.0 0.7 fusion.22
  214.8 0.1 mul.242
  214.9 0.6 fusion.39
  215.5 0.1 copy.48
  215.6 0.1 copy.46
  215.6 0.2 fusion.26
  215.8 76.1 %all-gather.5.cloned.1.call-done = bf16[16,1032,128]{2,1,0:T(8,128)(2,1)} async-done(((bf16[1,1032,128]{2,1,0:T(8,128)(2,1)}), bf16[16,1032,128]{2,1,0:T(8,128)(2,1)}) %all-gather.5.cloned.1.call-update) | async-done | bytes 4227088 | tf_op jit(solution)/shard_map/all_gather | solution.py:47
  292.0 0.8 slice_convert_fusion
  292.7 0.1 select_reduce_fusion
  292.9 0.1 select_bitcast_fusion
  292.9 0.1 copy.51
  293.0 2.2 slice-done
  295.2 3.6 %fusion = f32[16,1,64,128]{3,1,2,0:T(1,128)S(1)} fusion(f32[16,16,1,1]{0,2,3,1:T(1,128)S(1)} %copy.51, bf16[16,16,64,128]{3,2,1,0:T(8,128)(2,1)S(1)} %bitcast.100), kind=kOutput, calls=%fused_computation.1 | convolution fusion | flops 25165824 | bytes 4719616 | tf_op jit(solution)/shard_map/jgh,jghpn->ghpn/dot_general | solution.py:56
  298.8 0.4 fusion.8
  299.1 0.6 multiply_reduce_fusion
  299.8 0.2 multiply_convert_fusion.4
  300.0 0.9 copy.50
  (53 shorter events, 0.5 us)
Async XLA Ops:
  7.2 170.5 %all-gather.3.cloned.1.call-start = ((), (), s32[]{:S(2)}) async-start(), calls=%async_computation | async-start | bytes 10649600 | tf_op jit(solution)/shard_map/all_gather | solution.py:111
  9.6 282.3 %all-gather.5.cloned.1.call-start = ((), (), s32[]{:S(2)}) async-start(), calls=%async_computation.1 | async-start | bytes 4491264 | tf_op jit(solution)/shard_map/all_gather | solution.py:47
  9.7 51.8 %copy-start.1 = (f32[5,1024]{1,0:T(8,128)S(1)}, f32[5,1024]{1,0:T(8,128)}, u32[]{:S(2)}) copy-start(f32[5,1024]{1,0:T(8,128)} %param.16) | copy-start | bytes 61444
  9.7 51.8 %copy-start.3 = (f32[5,128]{1,0:T(8,128)S(1)}, f32[5,128]{1,0:T(8,128)}, u32[]{:S(2)}) copy-start(f32[5,128]{1,0:T(8,128)} %param.17) | copy-start | bytes 7684
  61.6 127.7 %copy-start.5 = (f32[16]{0:T(128)S(1)}, f32[16]{0:T(128)}, u32[]{:S(2)}) copy-start(f32[16]{0:T(128)} %param.19) | copy-start | bytes 196
  61.6 133.2 %copy-start.4 = (f32[16]{0:T(128)S(1)}, f32[16]{0:T(128)}, u32[]{:S(2)}) copy-start(f32[16]{0:T(128)} %param.18) | copy-start | bytes 196
  185.7 29.1 %copy-start.2 = (f32[1024]{0:T(1024)S(1)}, f32[1024]{0:T(1024)}, u32[]{:S(2)}) copy-start(f32[1024]{0:T(1024)} %param.21) | copy-start | bytes 12292
  185.8 7.5 %collective-permute-start = (bf16[3,1152]{0,1:T(8,128)(2,1)S(1)}, bf16[3,1152]{0,1:T(8,128)(2,1)S(1)}, u32[]{:S(2)}, u32[]{:S(2)}) collective-permute-start(bf16[3,1152]{0,1:T(8,128)(2,1)S(1)} %slice.123), channel_id=1, source_target_pairs={{0,8},{8,16},{16,24},{24,32},{32,40},{40,48},{48,56},{56,64},{64,7... | collective-permute-start | bytes 20744 | tf_op jit(solution)/shard_map/ppermute | solution.py:38
  194.7 98.3 %copy-start = (bf16[128,1152]{0,1:T(8,128)(2,1)}, bf16[128,1152]{0,1:T(8,128)(2,1)S(1)}, u32[]{:S(2)}) copy-start(bf16[128,1152]{0,1:T(8,128)(2,1)S(1)} %multiply_convert_fusion.2) | copy-start | bytes 884740
  194.8 4.6 %collective-permute-start.1 = (bf16[128,128]{0,1:T(8,128)(2,1)S(1)}, bf16[128,128]{0,1:T(8,128)(2,1)S(1)}, u32[]{:S(2)}, u32[]{:S(2)}) collective-permute-start(bf16[128,128]{0,1:T(8,128)(2,1)S(1)} %slice.133), channel_id=1, source_target_pairs={{0,1},{1,2},{2,3},{3,4},{4,5},{5,6},{6,7},{7,0},{8,9},{9,10},{10,1... | collective-permute-start | bytes 98312 | tf_op jit(solution)/shard_map/ppermute | solution.py:26
  199.3 4.6 %collective-permute-start.2 = (bf16[128,128]{0,1:T(8,128)(2,1)S(1)}, bf16[128,128]{0,1:T(8,128)(2,1)S(1)}, u32[]{:S(2)}, u32[]{:S(2)}) collective-permute-start(bf16[128,128]{0,1:T(8,128)(2,1)S(1)} %collective-permute-done.1), channel_id=1, source_target_pairs={{0,1},{1,2},{2,3},{3,4},{4,5},{5,6},{6,7},{7,0},{8,9},{9,10},{10,1... | collective-permute-start | bytes 98312 | tf_op jit(solution)/shard_map/ppermute | solution.py:26
  199.4 4.6 %collective-permute-start.5 = (bf16[128,128]{0,1:T(8,128)(2,1)S(1)}, bf16[128,128]{0,1:T(8,128)(2,1)S(1)}, u32[]{:S(2)}, u32[]{:S(2)}) collective-permute-start(bf16[128,128]{0,1:T(8,128)(2,1)S(1)} %slice.133), channel_id=1, source_target_pairs={{1,0},{2,1},{3,2},{4,3},{5,4},{6,5},{7,6},{0,7},{9,8},{10,9},{11,1... | collective-permute-start | bytes 98312 | tf_op jit(solution)/shard_map/ppermute | solution.py:28
  203.9 4.6 %collective-permute-start.3 = (bf16[128,128]{0,1:T(8,128)(2,1)S(1)}, bf16[128,128]{0,1:T(8,128)(2,1)S(1)}, u32[]{:S(2)}, u32[]{:S(2)}) collective-permute-start(bf16[128,128]{0,1:T(8,128)(2,1)S(1)} %collective-permute-done.2), channel_id=1, source_target_pairs={{0,1},{1,2},{2,3},{3,4},{4,5},{5,6},{6,7},{7,0},{8,9},{9,10},{10,1... | collective-permute-start | bytes 98312 | tf_op jit(solution)/shard_map/ppermute | solution.py:26
  204.0 4.6 %collective-permute-start.6 = (bf16[128,128]{0,1:T(8,128)(2,1)S(1)}, bf16[128,128]{0,1:T(8,128)(2,1)S(1)}, u32[]{:S(2)}, u32[]{:S(2)}) collective-permute-start(bf16[128,128]{0,1:T(8,128)(2,1)S(1)} %collective-permute-done.5), channel_id=1, source_target_pairs={{1,0},{2,1},{3,2},{4,3},{5,4},{6,5},{7,6},{0,7},{9,8},{10,9},{11,1... | collective-permute-start | bytes 98312 | tf_op jit(solution)/shard_map/ppermute | solution.py:28
  208.4 4.6 %collective-permute-start.4 = (bf16[128,128]{0,1:T(8,128)(2,1)S(1)}, bf16[128,128]{0,1:T(8,128)(2,1)S(1)}, u32[]{:S(2)}, u32[]{:S(2)}) collective-permute-start(bf16[128,128]{0,1:T(8,128)(2,1)S(1)} %collective-permute-done.3), channel_id=1, source_target_pairs={{0,1},{1,2},{2,3},{3,4},{4,5},{5,6},{6,7},{7,0},{8,9},{9,10},{10,1... | collective-permute-start | bytes 98312 | tf_op jit(solution)/shard_map/ppermute | solution.py:26
  208.6 4.6 %collective-permute-start.7 = (bf16[128,128]{0,1:T(8,128)(2,1)S(1)}, bf16[128,128]{0,1:T(8,128)(2,1)S(1)}, u32[]{:S(2)}, u32[]{:S(2)}) collective-permute-start(bf16[128,128]{0,1:T(8,128)(2,1)S(1)} %collective-permute-done.6), channel_id=1, source_target_pairs={{1,0},{2,1},{3,2},{4,3},{5,4},{6,5},{7,6},{0,7},{9,8},{10,9},{11,1... | collective-permute-start | bytes 98312 | tf_op jit(solution)/shard_map/ppermute | solution.py:28
  293.0 2.2 slice-start
  293.0 6.1 %copy-start.6 = (f32[16]{0:T(128)S(1)}, f32[16]{0:T(128)}, u32[]{:S(2)}) copy-start(f32[16]{0:T(128)} %param.20) | copy-start | bytes 196
  295.2 4.0 %slice-start.1 = ((bf16[128,1152]{0,1:T(8,128)(2,1)}), bf16[128,1024]{0,1:T(8,128)(2,1)S(1)}, s32[]{:S(2)}) async-start(bf16[128,1152]{0,1:T(8,128)(2,1)} %copy-done), calls=%async_computation.3 | async-start | bytes 524288 | tf_op jit(solution)/shard_map/slice | solution.py:129
Sparse Core Ops, SparseCore 0:
  11.5 166.0 all-gather.2
  214.9 77.0 all-gather.4
